TPU v7x, 32 devices: a whole 2x2x4 slice. The times are simulated.
32 devices in a mesh: seq: 8 (over z, y), exp: 4 (over x, core).
Axes of the slice: x: 2, y: 2, z: 4, core: 2. Of those that a mesh axis runs over, the one named last changes fastest.
Arguments:
- hidden: bfloat16 [4, 1024, 2048], P('exp', 'seq'), may hold values from -6 to 6
- lengths: int32 [4, 4], P('exp'), may hold values from 1 to 512, 1024 in all within a row
- attn_gain: float32 [2048], replicated, may hold values from 0 to 10
- w_qkv: bfloat16 [2048, 3, 16, 128], P(None, None, 'seq'), may hold values from -0.125 to 0.125
- w_out: bfloat16 [16, 128, 2048], P('seq'), may hold values from -0.125 to 0.125
- moe_gain: float32 [2048], replicated, may hold values from 0.5 to 1.5
- router: bfloat16 [2048, 16], replicated, may hold values from -8 to 8
- routes: int32 [4, 1024, 6], P('exp', 'seq'), may hold values from 0 to 15, all different within a row; in each aligned block of 128 rows (0 to 127, 128 to 255, ..., all dimensions but the last counted through in order) at most 56 rows name the same one
- w_gate_up: bfloat16 [32, 2, 704, 2048], P(('seq', 'exp')), may hold values from -0.125 to 0.125
- w_down: bfloat16 [32, 704, 2048], P(('seq', 'exp')), may hold values from -0.15625 to 0.15625
- final_gain: float32 [2048], replicated, may hold values from 0.5 to 1.5
- lm_head: bfloat16 [102400, 2048], P(('seq', 'exp')), may hold values from -4 to 4
Outputs:
- layer_out: bfloat16 [4, 1024, 2048], P('exp', 'seq')
- logprobs: float32 [16, 102400], P(None, ('seq', 'exp'))
Inputs may be any that keep to these rules, and one draw needn't show every extreme that they name: `routes`: in the rows of one device no expert is named by more than 56 rows; in some devices one expert is named by exactly 56 rows. `lengths`: each row sums to 1024; its largest entry is 512.
All inputs are finite; a program needn't handle non-finite values.
Results may differ from a plain program's by a relative error of at most 0.0095.
The roundings to bfloat16 on the way count: a program that leaves them out, or rounds other values in their place, can miss the bound.
Values may be sent and summed in bfloat16 or wider, within the bound.
No kernel may reach another device: no remote copies, remote signals or barrier semaphores. Data moves between devices by JAX's collectives and lax.ppermute only.
A program may use at most 128 MiB of HBM per device.

v0:
```python
import jax
import jax.numpy as jnp
from jax import lax
from jax.sharding import PartitionSpec as P

epsilon = 1e-06


def joined(value, axis, join):
    pieces = jax.tree.map(lambda part: lax.all_gather(part, axis), value)
    head = jax.tree.map(lambda part: part[0], pieces)
    tail = jax.tree.map(lambda part: part[1:], pieces)
    subtotal, _ = lax.scan(lambda subtotal, piece: (join(subtotal, piece), None), head, tail)
    return subtotal


def rms_scale(values, gain):
    widened = values.astype(jnp.float32)
    inverse = lax.rsqrt(jnp.mean(widened * widened, axis=-1, keepdims=True) + epsilon)
    return widened * inverse * gain


def segment_layout(prompt_lengths, count):
    ends = jnp.cumsum(prompt_lengths)
    starts = ends - prompt_lengths
    places = jnp.arange(count, dtype=jnp.int32)
    member = ((places[:, None] >= starts[None, :]) & (places[:, None] < ends[None, :])).astype(
        jnp.int32
    )
    numbers = jnp.arange(prompt_lengths.shape[0], dtype=jnp.int32)
    segment = jnp.sum(member * numbers[None, :], axis=1)
    offset = places - jnp.sum(member * starts[None, :], axis=1)
    return (segment, offset)


def rotary(values, positions):
    half_size = values.shape[-1] // 2
    freqs = 10000.0 ** (-2.0 * jnp.arange(half_size, dtype=jnp.float32) / values.shape[-1])
    angles = positions.astype(jnp.float32)[:, None] * freqs[None, :]
    cosine = jnp.cos(angles)[:, None, :]
    sine = jnp.sin(angles)[:, None, :]
    first_half = values[..., :half_size]
    second_half = values[..., half_size:]
    return jnp.concatenate(
        [first_half * cosine - second_half * sine, second_half * cosine + first_half * sine],
        axis=-1,
    )


def pair_swap(value):
    count = lax.axis_size("exp")
    return lax.ppermute(value, "exp", [(i, i ^ 1) for i in range(count)])


def merge_softmax(earlier, later):
    highest = jnp.maximum(earlier[0], later[0])
    return (
        highest,
        earlier[1] * jnp.exp(earlier[0] - highest) + later[1] * jnp.exp(later[0] - highest),
    )


def per_device(
    hidden,
    lengths,
    attn_gain,
    w_qkv,
    w_out,
    moe_gain,
    router,
    routes,
    w_gate_up,
    w_down,
    final_gain,
    lm_head,
):
    seq_count = lax.axis_size("seq")
    group_count = lax.axis_size("exp")
    device_count = seq_count * group_count
    token_rows = hidden[0]
    tok_rows = token_rows.shape[0]
    model_width = token_rows.shape[1]
    group_tokens = tok_rows * seq_count
    head_count = w_qkv.shape[2]
    head_size = w_qkv.shape[3]
    scale_factor = head_size ** (-0.5)
    prompt_lengths = lengths[0]
    segment, offset = segment_layout(prompt_lengths, group_tokens)
    normed = rms_scale(token_rows, attn_gain).astype(jnp.bfloat16)
    qkv_weight = w_qkv.reshape(model_width, 3 * head_count * head_size)
    qkv = jnp.dot(
        lax.all_gather(normed, "seq", axis=0, tiled=True),
        qkv_weight,
        preferred_element_type=jnp.float32,
    ).reshape(group_tokens, 3, head_count, head_size)
    query = rotary(qkv[:, 0], offset).astype(jnp.bfloat16)
    keys = rotary(qkv[:, 1], offset).astype(jnp.bfloat16)
    values = qkv[:, 2].astype(jnp.bfloat16)
    block_rows = min(512, group_tokens)
    key_places = jnp.arange(group_tokens, dtype=jnp.int32)

    def one_block(block_index):
        first_row = block_index * block_rows
        block_query = lax.dynamic_slice_in_dim(query, first_row, block_rows, 0)
        block_segment = lax.dynamic_slice_in_dim(segment, first_row, block_rows, 0)
        query_places = first_row + jnp.arange(block_rows, dtype=jnp.int32)
        scores = (
            jnp.einsum("qhd,khd->hqk", block_query, keys, preferred_element_type=jnp.float32)
            * scale_factor
        )
        allowed = (block_segment[:, None] == segment[None, :]) & (
            key_places[None, :] <= query_places[:, None]
        )
        scores = jnp.where(allowed[None], scores, -1e30)
        highest = jnp.max(scores, axis=2, keepdims=True)
        weights = jnp.exp(scores - highest)
        probs = (weights / jnp.sum(weights, axis=2, keepdims=True)).astype(jnp.bfloat16)
        return jnp.einsum("hqk,khd->qhd", probs, values, preferred_element_type=jnp.float32).astype(
            jnp.bfloat16
        )

    blocks = lax.map(one_block, jnp.arange(group_tokens // block_rows, dtype=jnp.int32))
    heads_flat = blocks.reshape(group_tokens, head_count * head_size)
    regrouped = lax.all_to_all(heads_flat, "seq", split_axis=0, concat_axis=1, tiled=True)
    core = lax.axis_index("exp") % 2
    half_size = head_size // 2
    own_half = lax.dynamic_slice_in_dim(w_out, core * half_size, half_size, axis=1)
    own_weight = lax.all_gather(own_half, "seq", axis=0, tiled=True)
    other_weight = pair_swap(own_weight)
    regrouped = regrouped.reshape(tok_rows, -1, head_size)
    own_heads = lax.dynamic_slice_in_dim(regrouped, core * half_size, half_size, axis=2)
    other_heads = lax.dynamic_slice_in_dim(regrouped, (1 - core) * half_size, half_size, axis=2)
    mixed = jnp.einsum(
        "thd,hdo->to", own_heads, own_weight, preferred_element_type=jnp.float32
    ) + jnp.einsum("thd,hdo->to", other_heads, other_weight, preferred_element_type=jnp.float32)
    middle = (token_rows.astype(jnp.float32) + mixed).astype(jnp.bfloat16)
    expert_in = rms_scale(middle, moe_gain).astype(jnp.bfloat16)
    logits = jnp.dot(expert_in, router, preferred_element_type=jnp.float32)
    expert_count = router.shape[1]
    token_routes = routes[0]
    top_count = token_routes.shape[1]
    expert_ids = jnp.arange(expert_count, dtype=jnp.int32)
    chosen_mask = token_routes[:, :, None] == expert_ids[None, None, :]
    chosen = jnp.sum(jnp.where(chosen_mask, logits[:, None, :], 0.0), axis=2)
    gates = jax.nn.softmax(chosen, axis=-1)
    capacity = max(2, tok_rows * top_count * 7 // (6 * expert_count))
    flat_mask = chosen_mask.reshape(tok_rows * top_count, expert_count).astype(jnp.int32)
    earlier_count = jnp.cumsum(flat_mask, axis=0) - flat_mask
    slot_index = jnp.sum(earlier_count * flat_mask, axis=1)
    target = (token_routes.reshape(-1) * capacity + slot_index).reshape(tok_rows, top_count)
    slot_total = expert_count * capacity
    placed = target[:, :, None] == jnp.arange(slot_total, dtype=jnp.int32)[None, None, :]
    dispatch_table = jnp.any(placed, axis=1).astype(jnp.bfloat16)
    slot_weights = jnp.sum(jnp.where(placed, gates[:, :, None], 0.0), axis=1)
    packed = lax.dot_general(
        dispatch_table, expert_in, (((0,), (0,)), ((), ())), preferred_element_type=jnp.float32
    ).astype(jnp.bfloat16)
    shares = device_count // expert_count
    assert capacity % shares == 0
    outgoing = packed.reshape(device_count, capacity // shares, model_width)
    gate_up = w_gate_up[0]
    down_weight = w_down[0]
    other_gate_up = pair_swap(gate_up)
    other_down = pair_swap(down_weight)
    arrived = lax.all_to_all(outgoing, ("seq", "exp"), split_axis=0, concat_axis=0, tiled=True)
    arrived_shape = arrived.shape
    flat_rows = arrived.reshape(-1, model_width)

    def share_part(pair, down):
        both = jnp.einsum("rd,gfd->rgf", flat_rows, pair, preferred_element_type=jnp.float32)
        act = (jax.nn.silu(both[:, 0]) * both[:, 1]).astype(jnp.bfloat16)
        part = jnp.dot(act, down, preferred_element_type=jnp.float32).astype(jnp.bfloat16)
        return part.astype(jnp.float32)

    part_sum = share_part(gate_up, down_weight) + share_part(other_gate_up, other_down)
    returned = lax.all_to_all(
        part_sum.astype(jnp.bfloat16).reshape(arrived_shape),
        ("seq", "exp"),
        split_axis=0,
        concat_axis=0,
        tiled=True,
    )
    summed = returned.reshape(slot_total, model_width).astype(jnp.float32)
    routed = jnp.dot(
        slot_weights, summed, precision=lax.Precision.HIGHEST, preferred_element_type=jnp.float32
    )
    layer_rows = (middle.astype(jnp.float32) + routed).astype(jnp.bfloat16)
    prompt_count = prompt_lengths.shape[0]
    last_places = jnp.cumsum(prompt_lengths) - 1
    here_places = lax.axis_index("seq") * tok_rows + jnp.arange(tok_rows, dtype=jnp.int32)
    select_table = (last_places[:, None] == here_places[None, :]).astype(jnp.bfloat16)
    picked = jnp.dot(select_table, layer_rows, preferred_element_type=jnp.float32)
    board = jnp.zeros((group_count * prompt_count, model_width), jnp.bfloat16)
    board = lax.dynamic_update_slice_in_dim(
        board, picked.astype(jnp.bfloat16), lax.axis_index("exp") * prompt_count, 0
    )
    last_rows = lax.psum(board, ("seq", "exp")).astype(jnp.float32)
    final = rms_scale(last_rows, final_gain).astype(jnp.bfloat16)
    vocab_scores = lax.dot_general(
        final, lm_head, (((1,), (1,)), ((), ())), preferred_element_type=jnp.float32
    )
    local_peak = jnp.max(vocab_scores, axis=1)
    local_total = jnp.sum(jnp.exp(vocab_scores - local_peak[:, None]), axis=1)
    global_peak, global_total = joined((local_peak, local_total), ("seq", "exp"), merge_softmax)
    logprobs = vocab_scores - (global_peak + jnp.log(global_total))[:, None]
    return (layer_rows[None], logprobs)


def solution(mesh):
    return jax.shard_map(
        per_device,
        mesh=mesh,
        in_specs=(
            P("exp", "seq", None),
            P("exp", None),
            P(),
            P(None, None, "seq", None),
            P("seq", None, None),
            P(),
            P(),
            P("exp", "seq", None),
            P(("seq", "exp"), None, None, None),
            P(("seq", "exp"), None, None),
            P(),
            P(("seq", "exp"), None),
        ),
        out_specs=(P("exp", "seq", None), P(None, ("seq", "exp"))),
        check_vma=False,
    )
```

profile of v0, /device:TPU:0, one launch (start us, length us, event | category | flops | bytes accessed | tf_op | source)
XLA Modules:
  0.0 637.5 jit_solution(17529622819611426284)
XLA Ops:
  7.2 1.3 fusion.48
  8.6 2.1 fusion.50
  10.7 0.8 constant_dynamic-slice_fusion.2
  11.8 8.0 %reshape.269 = bf16[2048,768]{1,0:T(8,128)(2,1)} reshape(bf16[2048,3,2,128]{3,2,1,0:T(2,128)(2,1)} %param.19) | data formatting | bytes 6291456 | tf_op jit(solution)/shard_map/reshape | solution.py:90
  19.8 4.8 copy.43
  24.7 1.0 multiply_cosine_fusion
  25.7 61.2 %all-gather.5.cloned.1.call-done = bf16[1024,2048]{1,0:T(8,128)(2,1)} async-done(((bf16[128,2048]{1,0:T(8,128)(2,1)}), bf16[1024,2048]{1,0:T(8,128)(2,1)}) %all-gather.5.cloned.1.call-update) | async-done | bytes 4194320 | tf_op jit(solution)/shard_map/all_gather | solution.py:92
  86.9 6.2 fusion.31
  93.3 0.4 subtract_convert_fusion
  93.6 1.2 copy-done.4
  94.9 0.3 copy.45
  95.2 1.4 fusion.51
  96.6 0.3 copy.46
  96.8 64.4 %all-gather.7.cloned.1.call-done = bf16[16,64,2048]{2,1,0:T(8,128)(2,1)} async-done(((bf16[2,64,2048]{2,1,0:T(8,128)(2,1)}), bf16[16,64,2048]{2,1,0:T(8,128)(2,1)}) %all-gather.7.cloned.1.call-update) | async-done | bytes 4194320 | tf_op jit(solution)/shard_map/all_gather | solution.py:128
  161.3 17.8 %while.24 = (s32[]{:T(128)}, bf16[2,512,2,128]{3,2,1,0:T(2,128)(2,1)S(1)}, s32[2]{0:T(128)S(1)}, s32[1024]{0:T(1024)S(1)}, bf16[1024,2,128]{0,2,1:T(8,128)(2,1)S...) while((s32[]{:T(128)}, ...), condition=%wide.region_7.8_spmd.clone, body=%wide.region_4.7_spmd.clone.sunk | while | flops 544867840 | bytes 11557047 | solution.py:122
  161.3 0.6 dynamic_slice.72
  162.6 0.6 fusion.116
  163.2 3.7 fusion.117
  166.9 2.9 fusion.118
  169.9 0.3 copy_dynamic-update-slice_fusion.2
  170.2 0.6 dynamic_slice.72
  171.5 0.6 fusion.116
  172.1 3.7 fusion.117
  175.8 2.9 fusion.118
  178.8 0.3 copy_dynamic-update-slice_fusion.2
  179.1 1.1 all_to_all.18
  180.2 3.7 all-to-all-start
  184.3 1.7 reduce-window.11
  186.1 0.3 slice_reduce_fusion
  186.7 0.5 fusion.33
  187.1 12.0 %all-to-all-done = bf16[8,128,256]{2,1,0:T(8,128)(2,1)S(1)} async-done(((bf16[8,128,256]{2,1,0:T(8,128)(2,1)}), bf16[8,128,256]{2,1,0:T(8,128)(2,1)S(1)}, u32[]{:S(2)}, u32[]{:S(2)}) %all-to-all-start) | async-done | bytes 524320 | tf_op jit(solution)/shard_map/all_to_all | solution.py:124
  199.1 0.3 copy.48
  199.4 2.9 convolution_bitcast_fusion.1
  202.4 3.1 multiply_reduce_fusion
  205.5 3.0 convolution_convert_fusion
  208.5 5.8 reshape.272
  214.3 3.7 all-to-all-start.1
  218.1 0.2 collective-permute-start.1
  218.3 0.3 collective-permute-start.2
  218.6 93.3 %all-to-all-done.1 = bf16[32,28,2048]{2,1,0:T(8,128)(2,1)} async-done(((bf16[32,28,2048]{2,1,0:T(8,128)(2,1)}), bf16[32,28,2048]{2,1,0:T(8,128)(2,1)}, u32[]{:S(2)}, u32[]{:S(2)}) %all-to-all-start.1) | async-done | bytes 3670048 | tf_op jit(solution)/shard_map/all_to_all | solution.py:165
  311.9 5.9 reshape.292
  317.8 9.4 %fusion.76 = f32[896,2,704]{0,2,1:T(8,128)S(1)} fusion(bf16[896,2048,1]{1,0,2:T(8,128)(2,1)} %reshape.292, bf16[1,2,704,2048]{3,2,1,0:T(8,128)(2,1)} %param.24), kind=kOutput, calls=%fused_computation.127 | convolution fusion | flops 5167382528 | bytes 14483456 | tf_op jit(solution)/shard_map/rd,gfd->rgf/dot_general | solution.py:170
  327.3 3.4 fusion.44
  330.7 8.4 %fusion.88 = f32[896,2,704]{0,2,1:T(8,128)S(1)} fusion(bf16[896,2048,1]{1,0,2:T(8,128)(2,1)S(1)} %copy-done.3, bf16[2,704,2048]{2,1,0:T(8,128)(2,1)} %collective-permute-done.1), kind=kOutput, calls=%fused_computation.134 | convolution fusion | flops 5167382528 | bytes 14483456 | tf_op jit(solution)/shard_map/rd,gfd->rgf/dot_general | solution.py:170
  339.2 6.9 %add_convert_fusion = bf16[896,2048]{1,0:T(8,128)(2,1)} fusion(bf16[896,2048]{1,0:T(8,128)(2,1)S(1)} %fusion.44, bf16[704,2048]{1,0:T(8,128)(2,1)} %collective-permute-done.2, f32[896,2,704]{0,2,1:T(8,128)S(1)} %fusion.88), kind=kOutput, calls=%fused_computation.31 | convolution fusion | flops 2596651008 | bytes 15269888 | tf_op jit(solution)/shard_map/dot_general | solution.py:172
  346.0 5.8 reshape.274
  351.9 4.1 all-to-all-start.2
  356.0 0.3 all-reduce.5.cloned.1.call-start
  356.3 0.3 fusion.80
  356.7 0.4 select_reduce_fusion
  357.1 92.8 %all-to-all-done.2 = bf16[32,28,2048]{2,1,0:T(8,128)(2,1)} async-done(((bf16[32,28,2048]{2,1,0:T(8,128)(2,1)}), bf16[32,28,2048]{2,1,0:T(8,128)(2,1)}, u32[]{:S(2)}, u32[]{:S(2)}) %all-to-all-start.2) | async-done | bytes 3670048 | tf_op jit(solution)/shard_map/all_to_all | solution.py:176
  449.8 5.8 reshape.275
  455.7 3.9 fusion.40
  459.6 0.2 fusion.42
  459.8 0.6 copy-done.6
  460.5 117.0 %all-reduce.5.cloned.1.call-done = bf16[16,2048]{1,0:T(8,128)(2,1)} async-done(((bf16[16,2048]{1,0:T(8,128)(2,1)}), bf16[16,2048]{1,0:T(8,128)(2,1)}) %all-reduce.5.cloned.1.call-update) | async-done | bytes 65552 | tf_op jit(solution)/shard_map/psum | solution.py:197
  577.5 1.0 fusion.54
  578.5 8.5 %fusion.87 = (f32[16]{0:T(128)S(1)}, f32[16,3200]{1,0:T(8,128)S(1)}) fusion(bf16[3200,2048]{1,0:T(8,128)(2,1)} %param.27, bf16[16,2048]{1,0:T(8,128)(2,1)} %all-reduce.5.cloned.1.call-done, f32[2048]{0:T(1024)S(1)} %copy-done.10, f32[16]{0:T(128)S(1)} %add_rsqrt_fusion), kind=kOutput, calls=%fused_computation.133 | convolution fusion | flops 209897456 | bytes 13385856 | tf_op jit(solution)/shard_map/dot_general | solution.py:199
  587.0 0.2 exponential_reduce_fusion
  587.2 0.2 dynamic-update-slice
  587.5 0.2 dynamic-update-slice.1
  587.7 40.8 %all-reduce.2 = (f32[512]{0:T(512)S(1)}, f32[512]{0:T(512)S(1)}) all-reduce(f32[512]{0:T(512)S(1)} %dynamic-update-slice, f32[512]{0:T(512)S(1)} %dynamic-update-slice.1), channel_id=2, replica_groups=mesh['seq'=8,'exp'=4] {'seq','exp'}, use_global_device_ids=true, to_apply=%add | all-reduce | flops 1024 | bytes 8192
  628.8 1.3 while.23
  630.2 0.8 broadcast_subtract_fusion
  (106 shorter events, 2.9 us)
Async XLA Ops:
  7.2 3.5 copy-start
  7.2 4.4 copy-start.12
  7.2 79.7 %all-gather.5.cloned.1.call-start = ((), (), s32[]{:S(2)}) async-start(), calls=%async_computation.3 | async-start | bytes 4718592 | tf_op jit(solution)/shard_map/all_gather | solution.py:92
  10.6 150.7 %all-gather.7.cloned.1.call-start = ((), (), s32[]{:S(2)}) async-start(), calls=%async_computation.4 | async-start | bytes 4718592 | tf_op jit(solution)/shard_map/all_gather | solution.py:128
  93.1 1.7 copy-start.4
  161.3 41.1 %collective-permute-start = (bf16[16,64,2048]{2,1,0:T(8,128)(2,1)}, bf16[16,64,2048]{2,1,0:T(8,128)(2,1)}, u32[]{:S(2)}, u32[]{:S(2)}) collective-permute-start(bf16[16,64,2048]{2,1,0:T(8,128)(2,1)} %all-gather.7.cloned.1.call-done), channel_id=1, source_target_pairs={{0,1},{1,0},{2,3},{3,2},{4,5},{5,4},{6,7},{7,6},{8,9},{9,8},{10,11... | collective-permute-start | bytes 12582920 | tf_op jit(solution)/shard_map/ppermute | solution.py:52
  161.3 22.6 %copy-start.9 = (s32[1,128,6]{1,0,2:T(1,128)S(1)}, s32[1,128,6]{1,0,2:T(1,128)}, u32[]{:S(2)}) copy-start(s32[1,128,6]{1,0,2:T(1,128)} %param.23) | copy-start | bytes 9220
  180.2 18.9 %all-to-all-start = ((bf16[8,128,256]{2,1,0:T(8,128)(2,1)}), bf16[8,128,256]{2,1,0:T(8,128)(2,1)S(1)}, u32[]{:S(2)}, u32[]{:S(2)}) async-start(bf16[8,128,256]{2,1,0:T(8,128)(2,1)} %all_to_all.18), calls=%async_computation | async-start | bytes 1048576 | tf_op jit(solution)/shard_map/all_to_all | solution.py:124
  184.2 18.2 %copy-start.2 = (bf16[1,128,2048]{2,1,0:T(8,128)(2,1)S(1)}, bf16[1,128,2048]{2,1,0:T(8,128)(2,1)}, u32[]{:S(2)}) copy-start(bf16[1,128,2048]{2,1,0:T(8,128)(2,1)} %param.16) | copy-start | bytes 1572868
  202.4 3.1 copy-start.8
  214.3 97.6 %all-to-all-start.1 = ((bf16[32,28,2048]{2,1,0:T(8,128)(2,1)}), bf16[32,28,2048]{2,1,0:T(8,128)(2,1)}, u32[]{:S(2)}, u32[]{:S(2)}) async-start(bf16[32,28,2048]{2,1,0:T(8,128)(2,1)} %reshape.272), calls=%async_computation.1 | async-start | bytes 8388608 | tf_op jit(solution)/shard_map/all_to_all | solution.py:165
  218.1 112.7 %collective-permute-start.1 = (bf16[2,704,2048]{2,1,0:T(8,128)(2,1)}, bf16[2,704,2048]{2,1,0:T(8,128)(2,1)}, u32[]{:S(2)}, u32[]{:S(2)}) collective-permute-start(bf16[2,704,2048]{2,1,0:T(8,128)(2,1)} %bitcast.143), channel_id=1, source_target_pairs={{0,1},{1,0},{2,3},{3,2},{4,5},{5,4},{6,7},{7,6},{8,9},{9,8},{10,11... | collective-permute-start | bytes 17301512 | tf_op jit(solution)/shard_map/ppermute | solution.py:52
  218.3 120.9 %collective-permute-start.2 = (bf16[704,2048]{1,0:T(8,128)(2,1)}, bf16[704,2048]{1,0:T(8,128)(2,1)}, u32[]{:S(2)}, u32[]{:S(2)}) collective-permute-start(bf16[704,2048]{1,0:T(8,128)(2,1)} %bitcast.144), channel_id=1, source_target_pairs={{0,1},{1,0},{2,3},{3,2},{4,5},{5,4},{6,7},{7,6},{8,9},{9,8},{10,11... | collective-permute-start | bytes 8650760 | tf_op jit(solution)/shard_map/ppermute | solution.py:52
  317.8 9.4 %copy-start.11 = (bf16[1,704,2048]{2,1,0:T(8,128)(2,1)S(1)}, bf16[1,704,2048]{2,1,0:T(8,128)(2,1)}, u32[]{:S(2)}) copy-start(bf16[1,704,2048]{2,1,0:T(8,128)(2,1)} %param.25) | copy-start | bytes 8650756
  327.3 3.4 copy-start.3
  351.9 4.4 copy-start.7
  351.9 98.0 %all-to-all-start.2 = ((bf16[32,28,2048]{2,1,0:T(8,128)(2,1)}), bf16[32,28,2048]{2,1,0:T(8,128)(2,1)}, u32[]{:S(2)}, u32[]{:S(2)}) async-start(bf16[32,28,2048]{2,1,0:T(8,128)(2,1)} %reshape.274), calls=%async_computation.2 | async-start | bytes 8388608 | tf_op jit(solution)/shard_map/all_to_all | solution.py:176
  356.0 221.6 %all-reduce.5.cloned.1.call-start = ((), (), s32[]{:S(2)}) async-start(), calls=%async_computation.5 | async-start | bytes 131072 | tf_op jit(solution)/shard_map/psum | solution.py:197
  455.7 122.8 %copy-start.10 = (f32[2048]{0:T(1024)S(1)}, f32[2048]{0:T(1024)}, u32[]{:S(2)}) copy-start(f32[2048]{0:T(1024)} %param.26) | copy-start | bytes 24580
  459.6 127.4 %copy-start.5 = (bf16[128,2048]{1,0:T(8,128)(2,1)}, bf16[128,2048]{1,0:T(8,128)(2,1)S(1)}, u32[]{:S(2)}) copy-start(bf16[128,2048]{1,0:T(8,128)(2,1)S(1)} %fusion.40) | copy-start | bytes 1572868
  459.8 0.6 copy-start.6
  578.5 52.4 %copy-start.1 = (bf16[2,128,2048]{2,1,0:T(8,128)(2,1)S(1)}, bf16[2,128,2048]{2,1,0:T(8,128)(2,1)}, u32[]{:S(2)}) copy-start(bf16[2,128,2048]{2,1,0:T(8,128)(2,1)} %param.20) | copy-start | bytes 3145732
Sparse Core Ops, SparseCore 0:
  10.7 76.0 all-gather.4
  89.6 71.6 all-gather.6
  460.6 116.8 all-reduce.4
where the time goes:
time: 639 us; the launch traced here: 637 us
  waiting for transfers between devices  441 us (69%)
  matrix products  69.6 us (11%)
  local copies, waits for them, and re-layouts  45.9 us (7%)
  blocking collectives  40.8 us (6%)
  between operations  14.3 us (2%)
  starting transfers between devices  12.4 us (2%)
  other arithmetic  11.9 us (2%)
    psum x1, waiting for transfers between devices, per_device(): last_rows = lax.psum(board, ('seq', 'exp')).astype(jnp.float32)  117 us
    all_to_all x1, waiting for transfers between devices, per_device(): lax.all_to_all(outgoing, ('seq', 'exp'), split_axis=0, concat_axis=0, til...  93.3 us
    all_to_all x1, waiting for transfers between devices, per_device(): lax.all_to_all(part_sum.astype(jnp.bfloat16).reshape(arrived_shape), ('se...  92.8 us
    all_gather x1, waiting for transfers between devices, per_device(): own_weight = lax.all_gather(own_half, 'seq', axis=0, tiled=True)  64.4 us
    all_gather x1, waiting for transfers between devices, per_device(): lax.all_gather(normed, 'seq', axis=0, tiled=True)  61.2 us
    unnamed x1, blocking collectives  40.8 us
    dot_general x2, matrix products, share_part(): jnp.einsum('rd,gfd->rgf', flat_rows, pair, preferred_element_type=jnp.flo...  17.8 us
  transfers between devices with their start and end apart: 9, of which 6 were waited for; matrix products, arithmetic and copies ran while one was open for 12% of the time, Pallas kernels for 0%

commit v1 on v0

--- a/solution.py
+++ b/solution.py
@@ -4,6 +4,12 @@
 from jax.sharding import PartitionSpec as P
 
 epsilon = 1e-06
+
+
+def in_order(blocks, dim):
+    blocks = jnp.moveaxis(blocks, 0, dim)
+    shape = blocks.shape
+    return blocks.reshape(*shape[:dim], shape[dim] * shape[dim + 1], *shape[dim + 2 :])
 
 
 def joined(value, axis, join):
@@ -125,7 +131,19 @@
     core = lax.axis_index("exp") % 2
     half_size = head_size // 2
     own_half = lax.dynamic_slice_in_dim(w_out, core * half_size, half_size, axis=1)
-    own_weight = lax.all_gather(own_half, "seq", axis=0, tiled=True)
+    peers = lax.axis_size("seq")
+    pairs = [(i_2, (i_2 + 1) % peers) for i_2 in range(peers)]
+    back = [(b, a) for a, b in pairs]
+    lower, upper = ([], [])
+    for lap in range(peers - 1):
+        if lap % 2 == 0:
+            lower.append(lax.ppermute(lower[-1] if lower else own_half, "seq", pairs))
+        else:
+            upper.append(lax.ppermute(upper[-1] if upper else own_half, "seq", back))
+    blocks_2 = jnp.stack([*lower[::-1], own_half, *upper])
+    shift = lax.axis_index("seq") - len(lower)
+    blocks_2 = blocks_2[(jnp.arange(peers) - shift) % peers]
+    own_weight = in_order(blocks_2, 0)
     other_weight = pair_swap(own_weight)
     regrouped = regrouped.reshape(tok_rows, -1, head_size)
     own_heads = lax.dynamic_slice_in_dim(regrouped, core * half_size, half_size, axis=2)

time: 639 us -> 627 us (0.981)
  waiting for transfers between devices: 441 us -> 377 us
  starting transfers between devices: 12.4 us -> 53.7 us
  local copies, waits for them, and re-layouts: 45.9 us -> 57.6 us
    all_gather x1 -> x0, waiting for transfers between devices: 64.4 us -> none  [per_device(): own_weight = lax.all_gather(own_half, 'seq', axis=0, tiled=True)]
    ppermute x0 -> x7, waiting for transfers between devices: none -> 62.1 us  [the longest x4 62.1 us: per_device(): lower.append(lax.ppermute(lower[-1] if lower else own_half, 'seq', pairs))]
    all_gather x1, waiting for transfers between devices: 61.2 us -> 0.01 us  [per_device(): lax.all_gather(normed, 'seq', axis=0, tiled=True)]
    ppermute x0 -> x7, starting transfers between devices: none -> 38.8 us  [the longest x3 33.3 us: per_device(): upper.append(lax.ppermute(upper[-1] if upper else own_half, 'seq', back))]
    unnamed x33 -> x44, local copies, waits for them, and re-layouts: 2.96 us -> 12 us
  transfers between devices with their start and end apart: 9 -> 15, of which waited for: 6 -> 8; matrix products, arithmetic and copies ran while one was open for 12% -> 13% of each run, Pallas kernels for 0% -> 0%
where the time goes in v1:
time: 627 us; the launch traced here: 625 us
  waiting for transfers between devices  377 us (60%)
  matrix products  66.4 us (11%)
  local copies, waits for them, and re-layouts  57.6 us (9%)
  starting transfers between devices  53.7 us (9%)
  blocking collectives  40.8 us (7%)
  between operations  14.6 us (2%)
  other arithmetic  13.2 us (2%)
    psum x1, waiting for transfers between devices, per_device(): last_rows = lax.psum(board, ('seq', 'exp')).astype(jnp.float32)  117 us
    all_to_all x1, waiting for transfers between devices, per_device(): lax.all_to_all(outgoing, ('seq', 'exp'), split_axis=0, concat_axis=0, til...  93.3 us
    all_to_all x1, waiting for transfers between devices, per_device(): lax.all_to_all(part_sum.astype(jnp.bfloat16).reshape(arrived_shape), ('se...  92.8 us
    ppermute x4, waiting for transfers between devices, per_device(): lower.append(lax.ppermute(lower[-1] if lower else own_half, 'seq', pairs))  62.1 us
    unnamed x1, blocking collectives  40.8 us
    ppermute x3, starting transfers between devices, per_device(): upper.append(lax.ppermute(upper[-1] if upper else own_half, 'seq', back))  33.3 us
    dot_general x2, matrix products, share_part(): jnp.einsum('rd,gfd->rgf', flat_rows, pair, preferred_element_type=jnp.flo...  17.8 us
  transfers between devices with their start and end apart: 15, of which 8 were waited for; matrix products, arithmetic and copies ran while one was open for 13% of the time, Pallas kernels for 0%

profile of v1, /device:TPU:0, one launch (start us, length us, event | category | flops | bytes accessed | tf_op | source)
XLA Modules:
  0.0 625.3 jit_solution(1628489898753885138)
XLA Ops:
  7.2 1.2 fusion.48
  8.5 2.0 fusion.50
  10.5 1.9 constant_dynamic-slice_fusion.2
  12.4 3.0 collective-permute-start
  15.4 19.5 %collective-permute-done = bf16[2,64,2048]{2,1,0:T(8,128)(2,1)} collective-permute-done((bf16[2,64,2048]{2,1,0:T(8,128)(2,1)}, bf16[2,64,2048]{2,1,0:T(8,128)(2,1)}, u32[]{:S(2)}, u32[]{:S(2)}) %collective-permute-start) | collective-permute-done | bytes 524320 | tf_op jit(solution)/shard_map/ppermute | solution.py:140
  35.0 4.6 collective-permute-start.4
  39.6 0.8 reduce-window.10
  40.4 6.8 %reshape.321 = bf16[2048,768]{1,0:T(8,128)(2,1)S(1)} reshape(bf16[2048,3,2,128]{3,2,1,0:T(2,128)(2,1)} %param.19) | data formatting | bytes 6291456 | tf_op jit(solution)/shard_map/reshape | solution.py:96
  47.2 3.0 copy.32
  50.2 8.6 %collective-permute-done.1 = bf16[2,64,2048]{2,1,0:T(8,128)(2,1)} collective-permute-done((bf16[2,64,2048]{2,1,0:T(8,128)(2,1)}, bf16[2,64,2048]{2,1,0:T(8,128)(2,1)}, u32[]{:S(2)}, u32[]{:S(2)}) %collective-permute-start.1) | collective-permute-done | bytes 524320 | tf_op jit(solution)/shard_map/ppermute | solution.py:140
  59.0 11.4 %collective-permute-start.5 = (bf16[2,64,2048]{2,1,0:T(8,128)(2,1)}, bf16[2,64,2048]{2,1,0:T(8,128)(2,1)S(1)}, u32[]{:S(2)}, u32[]{:S(2)}) collective-permute-start(bf16[2,64,2048]{2,1,0:T(8,128)(2,1)} %collective-permute-done.4), channel_id=1, source_target_pairs={{4,0},{8,4},{12,8},{16,12},{20,16},{24,20},{28,24},{0,28},{5,1},{9... | collective-permute-start | bytes 1572872 | tf_op jit(solution)/shard_map/ppermute | solution.py:142
  70.4 22.2 %collective-permute-done.2 = bf16[2,64,2048]{2,1,0:T(8,128)(2,1)S(1)} collective-permute-done((bf16[2,64,2048]{2,1,0:T(8,128)(2,1)}, bf16[2,64,2048]{2,1,0:T(8,128)(2,1)S(1)}, u32[]{:S(2)}, u32[]{:S(2)}) %collective-permute-start.2) | collective-permute-done | bytes 524320 | tf_op jit(solution)/shard_map/ppermute | solution.py:140
  92.5 2.4 collective-permute-start.3
  94.9 1.8 multiply_cosine_fusion
  96.7 17.4 %collective-permute-start.6 = (bf16[2,64,2048]{2,1,0:T(8,128)(2,1)S(1)}, bf16[2,64,2048]{2,1,0:T(8,128)(2,1)S(1)}, u32[]{:S(2)}, u32[]{:S(2)}) collective-permute-start(bf16[2,64,2048]{2,1,0:T(8,128)(2,1)S(1)} %collective-permute-done.5), channel_id=1, source_target_pairs={{4,0},{8,4},{12,8},{16,12},{20,16},{24,20},{28,24},{0,28},{5,1},{9... | collective-permute-start | bytes 1572872 | tf_op jit(solution)/shard_map/ppermute | solution.py:142
  114.0 11.8 %collective-permute-done.3 = bf16[2,64,2048]{2,1,0:T(8,128)(2,1)S(1)} collective-permute-done((bf16[2,64,2048]{2,1,0:T(8,128)(2,1)S(1)}, bf16[2,64,2048]{2,1,0:T(8,128)(2,1)S(1)}, u32[]{:S(2)}, u32[]{:S(2)}) %collective-permute-start.3) | collective-permute-done | bytes 524320 | tf_op jit(solution)/shard_map/ppermute | solution.py:140
  125.8 0.9 bitcast_dynamic-update-slice_fusion.7
  126.7 0.9 bitcast_dynamic-update-slice_fusion.6
  127.6 1.9 bitcast_dynamic-update-slice_fusion.5
  129.5 1.9 bitcast_dynamic-update-slice_fusion.4
  131.4 0.9 bitcast_dynamic-update-slice_fusion.3
  132.3 1.9 bitcast_dynamic-update-slice_fusion.2
  134.2 0.8 bitcast_dynamic-update-slice_fusion.1
  135.0 0.8 bitcast_dynamic-update-slice_fusion
  135.9 5.1 gather_fusion
  141.0 5.3 fusion.31
  146.5 0.7 copy-done.6
  148.3 17.7 %while.24 = (s32[]{:T(128)}, bf16[2,512,2,128]{3,2,1,0:T(2,128)(2,1)S(1)}, s32[2]{0:T(128)S(1)}, s32[1024]{0:T(1024)S(1)}, bf16[1024,2,128]{0,2,1:T(8,128)(2,1)S...) while((s32[]{:T(128)}, ...), condition=%wide.region_7.8_spmd.clone, body=%wide.region_4.7_spmd.clone.sunk | while | flops 544867840 | bytes 11557047 | solution.py:128
  148.3 0.6 dynamic_slice.74
  149.6 0.6 fusion.118
  150.2 3.7 fusion.119
  153.9 2.9 fusion.120
  157.1 0.6 dynamic_slice.74
  158.5 0.6 fusion.118
  159.0 3.7 fusion.119
  162.7 2.9 fusion.120
  166.0 1.1 all_to_all.18
  167.1 6.1 all-to-all-start
  173.6 1.7 reduce-window.11
  175.9 0.5 fusion.33
  176.4 12.0 %all-to-all-done = bf16[8,128,256]{2,1,0:T(8,128)(2,1)S(1)} async-done(((bf16[8,128,256]{2,1,0:T(8,128)(2,1)}), bf16[8,128,256]{2,1,0:T(8,128)(2,1)S(1)}, u32[]{:S(2)}, u32[]{:S(2)}) %all-to-all-start) | async-done | bytes 524320 | tf_op jit(solution)/shard_map/all_to_all | solution.py:130
  188.7 3.1 convolution_bitcast_fusion
  192.1 0.9 multiply_reduce_fusion
  193.0 3.0 convolution_convert_fusion
  196.0 5.8 reshape.325
  201.8 3.8 all-to-all-start.1
  206.2 93.3 %all-to-all-done.1 = bf16[32,28,2048]{2,1,0:T(8,128)(2,1)} async-done(((bf16[32,28,2048]{2,1,0:T(8,128)(2,1)}), bf16[32,28,2048]{2,1,0:T(8,128)(2,1)}, u32[]{:S(2)}, u32[]{:S(2)}) %all-to-all-start.1) | async-done | bytes 3670048 | tf_op jit(solution)/shard_map/all_to_all | solution.py:183
  299.5 5.9 reshape.353
  305.5 9.4 %fusion.78 = f32[896,2,704]{0,2,1:T(8,128)S(1)} fusion(bf16[896,2048,1]{1,0,2:T(8,128)(2,1)} %reshape.353, bf16[1,2,704,2048]{3,2,1,0:T(8,128)(2,1)} %param.24), kind=kOutput, calls=%fused_computation.143 | convolution fusion | flops 5167382528 | bytes 14483456 | tf_op jit(solution)/shard_map/rd,gfd->rgf/dot_general | solution.py:188
  314.9 3.4 fusion.44
  318.4 8.4 %fusion.90 = f32[896,2,704]{0,2,1:T(8,128)S(1)} fusion(bf16[896,2048,1]{1,0,2:T(8,128)(2,1)S(1)} %copy-done.3, bf16[2,704,2048]{2,1,0:T(8,128)(2,1)} %collective-permute-done.8), kind=kOutput, calls=%fused_computation.150 | convolution fusion | flops 5167382528 | bytes 14483456 | tf_op jit(solution)/shard_map/rd,gfd->rgf/dot_general | solution.py:188
  326.8 6.9 %add_convert_fusion = bf16[896,2048]{1,0:T(8,128)(2,1)} fusion(bf16[896,2048]{1,0:T(8,128)(2,1)S(1)} %fusion.44, bf16[704,2048]{1,0:T(8,128)(2,1)} %collective-permute-done.9, f32[896,2,704]{0,2,1:T(8,128)S(1)} %fusion.90), kind=kOutput, calls=%fused_computation.32 | convolution fusion | flops 2596651008 | bytes 15269888 | tf_op jit(solution)/shard_map/dot_general | solution.py:190
  333.6 5.8 reshape.327
  339.5 4.1 all-to-all-start.2
  344.7 92.8 %all-to-all-done.2 = bf16[32,28,2048]{2,1,0:T(8,128)(2,1)} async-done(((bf16[32,28,2048]{2,1,0:T(8,128)(2,1)}), bf16[32,28,2048]{2,1,0:T(8,128)(2,1)}, u32[]{:S(2)}, u32[]{:S(2)}) %all-to-all-start.2) | async-done | bytes 3670048 | tf_op jit(solution)/shard_map/all_to_all | solution.py:194
  437.5 5.8 reshape.328
  443.3 3.9 fusion.40
  447.5 0.6 copy-done.9
  448.1 117.0 %all-reduce.5.cloned.1.call-done = bf16[16,2048]{1,0:T(8,128)(2,1)} async-done(((bf16[16,2048]{1,0:T(8,128)(2,1)}), bf16[16,2048]{1,0:T(8,128)(2,1)}) %all-reduce.5.cloned.1.call-update) | async-done | bytes 65552 | tf_op jit(solution)/shard_map/psum | solution.py:215
  565.1 1.0 fusion.54
  566.1 8.4 %fusion.89 = (f32[16]{0:T(128)S(1)}, f32[16,3200]{1,0:T(8,128)S(1)}) fusion(bf16[3200,2048]{1,0:T(8,128)(2,1)} %param.27, bf16[16,2048]{1,0:T(8,128)(2,1)} %all-reduce.5.cloned.1.call-done, f32[2048]{0:T(1024)S(1)} %copy-done.12, f32[16]{0:T(128)S(1)} %add_rsqrt_fusion), kind=kOutput, calls=%fused_computation.149 | convolution fusion | flops 209897456 | bytes 13385856 | tf_op jit(solution)/shard_map/dot_general | solution.py:217
  575.2 40.8 %all-reduce.2 = (f32[512]{0:T(512)S(1)}, f32[512]{0:T(512)S(1)}) all-reduce(f32[512]{0:T(512)S(1)} %dynamic-update-slice, f32[512]{0:T(512)S(1)} %dynamic-update-slice.1), channel_id=2, replica_groups=mesh['seq'=8,'exp'=4] {'seq','exp'}, use_global_device_ids=true, to_apply=%add | all-reduce | flops 1024 | bytes 8192
  616.3 1.3 while.23
  617.7 0.8 broadcast_subtract_fusion
  (132 shorter events, 7.7 us)
Async XLA Ops:
  7.2 336.7 %copy-start = (bf16[2048,16]{0,1:T(8,128)(2,1)S(1)}, bf16[2048,16]{0,1:T(8,128)(2,1)}, u32[]{:S(2)}) copy-start(bf16[2048,16]{0,1:T(8,128)(2,1)} %param.22) | copy-start | bytes 196612
  7.2 133.8 %all-gather.4.cloned.1.call-start = ((), (), s32[]{:S(2)}) async-start(), calls=%async_computation.3 | async-start | bytes 4718592 | tf_op jit(solution)/shard_map/all_gather | solution.py:98
  12.4 22.4 %collective-permute-start = (bf16[2,64,2048]{2,1,0:T(8,128)(2,1)}, bf16[2,64,2048]{2,1,0:T(8,128)(2,1)}, u32[]{:S(2)}, u32[]{:S(2)}) collective-permute-start(bf16[2,64,2048]{2,1,0:T(8,128)(2,1)} %constant_dynamic-slice_fusion.2), channel_id=1, source_target_pairs={{0,4},{4,8},{8,12},{12,16},{16,20},{20,24},{24,28},{28,0},{1,5},{5... | collective-permute-start | bytes 1572872 | tf_op jit(solution)/shard_map/ppermute | solution.py:140
  34.9 24.0 %collective-permute-start.1 = (bf16[2,64,2048]{2,1,0:T(8,128)(2,1)}, bf16[2,64,2048]{2,1,0:T(8,128)(2,1)}, u32[]{:S(2)}, u32[]{:S(2)}) collective-permute-start(bf16[2,64,2048]{2,1,0:T(8,128)(2,1)} %collective-permute-done), channel_id=1, source_target_pairs={{0,4},{4,8},{8,12},{12,16},{16,20},{20,24},{24,28},{28,0},{1,5},{5... | collective-permute-start | bytes 1572872 | tf_op jit(solution)/shard_map/ppermute | solution.py:140
  35.0 24.0 %collective-permute-start.4 = (bf16[2,64,2048]{2,1,0:T(8,128)(2,1)}, bf16[2,64,2048]{2,1,0:T(8,128)(2,1)}, u32[]{:S(2)}, u32[]{:S(2)}) collective-permute-start(bf16[2,64,2048]{2,1,0:T(8,128)(2,1)} %constant_dynamic-slice_fusion.2), channel_id=1, source_target_pairs={{4,0},{8,4},{12,8},{16,12},{20,16},{24,20},{28,24},{0,28},{5,1},{9... | collective-permute-start | bytes 1572872 | tf_op jit(solution)/shard_map/ppermute | solution.py:142
  47.2 11.6 %copy-start.14 = (s32[1,4]{1,0:T(1,128)S(1)}, s32[1,4]{1,0:T(1,128)}, u32[]{:S(2)}) copy-start(s32[1,4]{1,0:T(1,128)} %param.17) | copy-start | bytes 52
  50.2 81.2 %copy-start.7 = (bf16[2,128,2048]{2,1,0:T(8,128)(2,1)S(1)}, bf16[2,128,2048]{2,1,0:T(8,128)(2,1)}, u32[]{:S(2)}) copy-start(bf16[2,128,2048]{2,1,0:T(8,128)(2,1)} %param.20) | copy-start | bytes 3145732
  58.8 33.7 %collective-permute-start.2 = (bf16[2,64,2048]{2,1,0:T(8,128)(2,1)}, bf16[2,64,2048]{2,1,0:T(8,128)(2,1)S(1)}, u32[]{:S(2)}, u32[]{:S(2)}) collective-permute-start(bf16[2,64,2048]{2,1,0:T(8,128)(2,1)} %collective-permute-done.1), channel_id=1, source_target_pairs={{0,4},{4,8},{8,12},{12,16},{16,20},{20,24},{24,28},{28,0},{1,5},{5... | collective-permute-start | bytes 1572872 | tf_op jit(solution)/shard_map/ppermute | solution.py:140
  59.0 37.7 %collective-permute-start.5 = (bf16[2,64,2048]{2,1,0:T(8,128)(2,1)}, bf16[2,64,2048]{2,1,0:T(8,128)(2,1)S(1)}, u32[]{:S(2)}, u32[]{:S(2)}) collective-permute-start(bf16[2,64,2048]{2,1,0:T(8,128)(2,1)} %collective-permute-done.4), channel_id=1, source_target_pairs={{4,0},{8,4},{12,8},{16,12},{20,16},{24,20},{28,24},{0,28},{5,1},{9... | collective-permute-start | bytes 1572872 | tf_op jit(solution)/shard_map/ppermute | solution.py:142
  92.5 33.3 %collective-permute-start.3 = (bf16[2,64,2048]{2,1,0:T(8,128)(2,1)S(1)}, bf16[2,64,2048]{2,1,0:T(8,128)(2,1)S(1)}, u32[]{:S(2)}, u32[]{:S(2)}) collective-permute-start(bf16[2,64,2048]{2,1,0:T(8,128)(2,1)S(1)} %collective-permute-done.2), channel_id=1, source_target_pairs={{0,4},{4,8},{8,12},{12,16},{16,20},{20,24},{24,28},{28,0},{1,5},{5... | collective-permute-start | bytes 1572872 | tf_op jit(solution)/shard_map/ppermute | solution.py:140
  96.7 38.3 %collective-permute-start.6 = (bf16[2,64,2048]{2,1,0:T(8,128)(2,1)S(1)}, bf16[2,64,2048]{2,1,0:T(8,128)(2,1)S(1)}, u32[]{:S(2)}, u32[]{:S(2)}) collective-permute-start(bf16[2,64,2048]{2,1,0:T(8,128)(2,1)S(1)} %collective-permute-done.5), channel_id=1, source_target_pairs={{4,0},{8,4},{12,8},{16,12},{20,16},{24,20},{28,24},{0,28},{5,1},{9... | collective-permute-start | bytes 1572872 | tf_op jit(solution)/shard_map/ppermute | solution.py:142
  135.9 5.1 copy-start.4
  141.0 47.7 %collective-permute-start.7 = (bf16[16,64,2048]{2,1,0:T(8,128)(2,1)}, bf16[16,64,2048]{2,1,0:T(8,128)(2,1)}, u32[]{:S(2)}, u32[]{:S(2)}) collective-permute-start(bf16[16,64,2048]{2,1,0:T(8,128)(2,1)} %bitcast.153), channel_id=1, source_target_pairs={{0,1},{1,0},{2,3},{3,2},{4,5},{5,4},{6,7},{7,6},{8,9},{9,8},{10,11... | collective-permute-start | bytes 12582920 | tf_op jit(solution)/shard_map/ppermute | solution.py:58
  146.3 1.0 copy-start.6
  146.5 1.7 copy-start.8
  148.2 25.0 %copy-start.11 = (s32[1,128,6]{1,0,2:T(1,128)S(1)}, s32[1,128,6]{1,0,2:T(1,128)}, u32[]{:S(2)}) copy-start(s32[1,128,6]{1,0,2:T(1,128)} %param.23) | copy-start | bytes 9220
  167.1 24.6 %copy-start.2 = (bf16[1,128,2048]{2,1,0:T(8,128)(2,1)S(1)}, bf16[1,128,2048]{2,1,0:T(8,128)(2,1)}, u32[]{:S(2)}) copy-start(bf16[1,128,2048]{2,1,0:T(8,128)(2,1)} %param.16) | copy-start | bytes 1572868
  167.1 21.3 %all-to-all-start = ((bf16[8,128,256]{2,1,0:T(8,128)(2,1)}), bf16[8,128,256]{2,1,0:T(8,128)(2,1)S(1)}, u32[]{:S(2)}, u32[]{:S(2)}) async-start(bf16[8,128,256]{2,1,0:T(8,128)(2,1)} %all_to_all.18), calls=%async_computation | async-start | bytes 1048576 | tf_op jit(solution)/shard_map/all_to_all | solution.py:130
  188.6 3.5 copy-start.1
  192.1 0.9 copy-start.10
  201.8 97.7 %all-to-all-start.1 = ((bf16[32,28,2048]{2,1,0:T(8,128)(2,1)}), bf16[32,28,2048]{2,1,0:T(8,128)(2,1)}, u32[]{:S(2)}, u32[]{:S(2)}) async-start(bf16[32,28,2048]{2,1,0:T(8,128)(2,1)} %reshape.325), calls=%async_computation.1 | async-start | bytes 8388608 | tf_op jit(solution)/shard_map/all_to_all | solution.py:183
  205.7 112.7 %collective-permute-start.8 = (bf16[2,704,2048]{2,1,0:T(8,128)(2,1)}, bf16[2,704,2048]{2,1,0:T(8,128)(2,1)}, u32[]{:S(2)}, u32[]{:S(2)}) collective-permute-start(bf16[2,704,2048]{2,1,0:T(8,128)(2,1)} %bitcast.164), channel_id=1, source_target_pairs={{0,1},{1,0},{2,3},{3,2},{4,5},{5,4},{6,7},{7,6},{8,9},{9,8},{10,11... | collective-permute-start | bytes 17301512 | tf_op jit(solution)/shard_map/ppermute | solution.py:58
  205.9 120.9 %collective-permute-start.9 = (bf16[704,2048]{1,0:T(8,128)(2,1)}, bf16[704,2048]{1,0:T(8,128)(2,1)}, u32[]{:S(2)}, u32[]{:S(2)}) collective-permute-start(bf16[704,2048]{1,0:T(8,128)(2,1)} %bitcast.165), channel_id=1, source_target_pairs={{0,1},{1,0},{2,3},{3,2},{4,5},{5,4},{6,7},{7,6},{8,9},{9,8},{10,11... | collective-permute-start | bytes 8650760 | tf_op jit(solution)/shard_map/ppermute | solution.py:58
  305.5 9.4 %copy-start.13 = (bf16[1,704,2048]{2,1,0:T(8,128)(2,1)S(1)}, bf16[1,704,2048]{2,1,0:T(8,128)(2,1)}, u32[]{:S(2)}) copy-start(bf16[1,704,2048]{2,1,0:T(8,128)(2,1)} %param.25) | copy-start | bytes 8650756
  314.9 3.4 copy-start.3
  339.5 98.0 %all-to-all-start.2 = ((bf16[32,28,2048]{2,1,0:T(8,128)(2,1)}), bf16[32,28,2048]{2,1,0:T(8,128)(2,1)}, u32[]{:S(2)}, u32[]{:S(2)}) async-start(bf16[32,28,2048]{2,1,0:T(8,128)(2,1)} %reshape.327), calls=%async_computation.2 | async-start | bytes 8388608 | tf_op jit(solution)/shard_map/all_to_all | solution.py:194
  343.6 221.6 %all-reduce.5.cloned.1.call-start = ((), (), s32[]{:S(2)}) async-start(), calls=%async_computation.4 | async-start | bytes 131072 | tf_op jit(solution)/shard_map/psum | solution.py:215
  443.3 122.8 %copy-start.12 = (f32[2048]{0:T(1024)S(1)}, f32[2048]{0:T(1024)}, u32[]{:S(2)}) copy-start(f32[2048]{0:T(1024)} %param.26) | copy-start | bytes 24580
  447.2 127.3 %copy-start.5 = (bf16[128,2048]{1,0:T(8,128)(2,1)}, bf16[128,2048]{1,0:T(8,128)(2,1)S(1)}, u32[]{:S(2)}) copy-start(bf16[128,2048]{1,0:T(8,128)(2,1)S(1)} %fusion.40) | copy-start | bytes 1572868
  447.4 0.6 copy-start.9
Sparse Core Ops, SparseCore 0:
  10.6 129.3 all-gather.3
  448.2 116.8 all-reduce.4
